TPU v7x, 32 devices: a whole 2x2x4 slice. The times are simulated.
32 devices in a mesh: dp: 4 (over y, core), freq: 8 (over z, x).
Axes of the slice: x: 2, y: 2, z: 4, core: 2. Of those that a mesh axis runs over, the one named last changes fastest.
Arguments:
- grad_parts: float32 [4, 27, 4, 65536], P('dp', None, None, 'freq'), may hold values from -12 to 12
- kernel: float32 [27, 262144], P(None, ('dp', 'freq')), may hold values from -4 to 4
Outputs:
- clipped: float32 [27, 262144], P(None, ('dp', 'freq'))
All inputs are finite; a program needn't handle non-finite values.
Results may differ from a plain program's by a relative error of at most 0.0005.
The roundings to bfloat16 on the way count: a program that leaves them out, or rounds other values in their place, can miss the bound.
Values may be sent and summed in bfloat16 or wider, within the bound.
No kernel may reach another device: no remote copies, remote signals or barrier semaphores. Data moves between devices by JAX's collectives and lax.ppermute only.
A program may use at most 64 MiB of HBM per device.

v0:
```python
import math
import jax
import jax.numpy as jnp
from jax import lax
from jax.sharding import PartitionSpec as P

C = 512
TAPS = 27
GT = 8
GH = 32
GW = 32
KD = 2
CLIP = 0.25
HIGH = lax.Precision.HIGHEST


def tap_phases(freq_ids, stride):
    flat_index = freq_ids * stride
    freq_time = flat_index // (GH * GW)
    freq_row = flat_index // GW % GH
    freq_col = flat_index % GW
    taps = jnp.arange(TAPS, dtype=jnp.int32)
    off_time = taps // 9 - 1
    off_row = taps // 3 % 3 - 1
    off_col = taps % 3 - 1
    period = GT * GH * GW
    turns = (
        freq_time[:, None] * off_time[None, :] * (GH * GW)
        + freq_row[:, None] * off_row[None, :] * (GT * GW)
        + freq_col[:, None] * off_col[None, :] * (GT * GH)
    ) % period
    angle = turns.astype(jnp.float32) * (2.0 * math.pi / period)
    return (jnp.cos(angle), jnp.sin(angle))


def clip_factor(local_square):
    summed = lax.psum(local_square, ("dp", "freq"))
    return jnp.minimum(1.0, CLIP * math.sqrt(TAPS * C * C) / jnp.sqrt(summed + 1e-06))


def spectrum(field, cosine, sine_rows):
    real_spec = jnp.dot(cosine, field, precision=HIGH)
    imag_spec = -jnp.dot(sine_rows, field, precision=HIGH)
    return jnp.stack([real_spec, imag_spec], axis=1)


def taps_back(polar_part, cosine, sine_rows):
    values = polar_part.astype(jnp.float32)
    summed = jnp.dot(cosine.T, values[:, 0], precision=HIGH)
    return summed - jnp.dot(sine_rows.T, values[:, 1], precision=HIGH)


def polar_step(spectra):
    width = spectra.shape[-1]
    mean_square = jnp.mean(jnp.square(spectra.astype(jnp.float32)), axis=(1, 2, 3), keepdims=True)
    spread = math.sqrt(8.0 * width)
    scaled = (
        spectra.astype(jnp.float32) * (0.75 / (spread * jnp.sqrt(mean_square + 1e-06)))
    ).astype(jnp.bfloat16)
    real_part = scaled[:, 0]
    imag_part = scaled[:, 1]
    stacked = jnp.concatenate([real_part, imag_part], axis=1)
    turned = jnp.concatenate([imag_part, -real_part], axis=1)
    gram = jnp.einsum(
        "nri,nrj->nij",
        stacked,
        jnp.concatenate([stacked, turned], axis=2),
        preferred_element_type=jnp.float32,
    ).astype(jnp.bfloat16)
    gram_real = gram[:, :, :width]
    gram_imag = gram[:, :, width:]
    blocked = jnp.concatenate([gram, jnp.concatenate([-gram_imag, gram_real], axis=2)], axis=1)
    side = jnp.concatenate([real_part, imag_part], axis=2)
    product = jnp.einsum("nij,njk->nik", side, blocked, preferred_element_type=jnp.float32)
    result = (1.5 * side.astype(jnp.float32) - 0.5 * product).astype(jnp.bfloat16)
    return jnp.stack([result[:, :, :width], result[:, :, width:]], axis=1)


def on_device(grad_parts, kernel):
    devices_dp = lax.axis_size("dp")
    devices_freq = lax.axis_size("freq")
    total_freq = KD * devices_dp * devices_freq
    stride = GT * GH * GW // total_freq
    scale_out = math.sqrt(C / total_freq)
    own_width = kernel.shape[1]
    gradient = lax.psum_scatter(grad_parts[0], "dp", scatter_dimension=1, tiled=True).reshape(
        TAPS, own_width
    )
    local_square = jnp.sum(gradient * gradient)
    kernel_all, gradient_all = (kernel, gradient)
    freq_ids = jnp.arange(total_freq, dtype=jnp.int32)
    cosine, sine_rows = tap_phases(freq_ids, stride)
    factor = clip_factor(local_square)
    spectra = spectrum(kernel_all - factor * gradient_all, cosine, sine_rows)
    spectra = spectra.astype(jnp.bfloat16)
    count, row_width = (spectra.shape[0], spectra.shape[2])
    whole = lax.all_to_all(
        lax.all_to_all(
            spectra.reshape(count, 2, 1, 1, row_width),
            "dp",
            split_axis=0,
            concat_axis=2,
            tiled=True,
        ),
        "freq",
        split_axis=0,
        concat_axis=3,
        tiled=True,
    )
    polar_part = polar_step(whole.reshape(KD, 2, C, C))
    returned = lax.all_to_all(
        lax.all_to_all(
            polar_part.reshape(KD, 2, devices_dp, devices_freq, row_width),
            "dp",
            split_axis=2,
            concat_axis=0,
            tiled=True,
        ),
        "freq",
        split_axis=3,
        concat_axis=0,
        tiled=True,
    )
    position = jnp.arange(total_freq, dtype=jnp.int32)
    source_freq = position // (devices_dp * KD)
    source_dp = position // KD % devices_dp
    member = position % KD
    back_ids = source_dp * (devices_freq * KD) + source_freq * KD + member
    back_cos, back_sin = tap_phases(back_ids, stride)
    return taps_back(returned.reshape(count, 2, row_width), back_cos, back_sin) * scale_out


def solution(mesh):
    return jax.shard_map(
        on_device,
        mesh=mesh,
        in_specs=(P("dp", None, None, "freq"), P(None, ("dp", "freq"))),
        out_specs=P(None, ("dp", "freq")),
        check_vma=False,
    )
```

profile of v0, /device:TPU:0, one launch (start us, length us, event | category | flops | bytes accessed | tf_op | source)
XLA Modules:
  0.0 307.9 jit_solution(1594015570563499403)
XLA Ops:
  6.5 0.0 reduce-scatter.2.cloned.1.call-start
  6.5 6.0 %copy.47 = f32[1,27,4,8192]{3,1,2,0:T(8,128)} copy(f32[1,27,4,8192]{3,2,1,0:T(4,128)} %param.2) | data formatting | bytes 7077888 | tf_op args[0]
  12.5 0.0 copy-start.1
  12.5 0.0 reduce-scatter.2.cloned.1.call-update
  12.6 47.3 %reduce-scatter.2.cloned.1.call-done = f32[27,1,8192]{2,0,1:T(8,128)} async-done(((f32[27,4,8192]{2,0,1:T(8,128)}), f32[27,1,8192]{2,0,1:T(8,128)}) %reduce-scatter.2.cloned.1.call-update) | async-done | bytes 884752 | tf_op jit(solution)/shard_map/reduce_scatter | solution.py:86
  59.9 0.0 copy-start
  59.9 2.2 multiply_reduce_fusion.1
  62.1 39.5 %psum.7 = f32[]{:T(128)} all-reduce(f32[]{:T(128)} %multiply_reduce_fusion.1), channel_id=1, replica_groups=mesh['dp'=4,'freq'=8] {'dp','freq'}, use_global_device_ids=true, to_apply=%region_2.3 | all-reduce | flops 1 | bytes 8 | tf_op jit(solution)/shard_map/psum | solution.py:37
  102.3 0.0 copy-done.1
  102.3 3.2 %fusion.2 = bf16[64,1,1,1,8192]{4,0,3,2,1:T(8,128)(2,1)S(1)} fusion(f32[27,8192]{1,0:T(8,128)S(1)} %copy-done.1, f32[27,1,8192]{2,0,1:T(8,128)} %reduce-scatter.2.cloned.1.call-done, f32[]{:T(128)S(6)} %min_shard_map.3, s32[64]{0:T(128)S(1)} %get-tuple-element.11, s32[64]{0:T(128)S(1)} %get-tuple-element.12, s32[64]{0:T(128)S(1)} %and_select_fusion.3, ...), kind=kOutput, calls=%fused_computation.4 | convolution fusion | flops 171396544 | bytes 2819144 | tf_op jit(solution)/shard_map/dot_general | solution.py:43
  105.6 0.0 copy-done
  105.6 2.0 fusion.1
  107.6 0.2 pad_maximum_fusion
  107.8 2.2 copy.32
  110.0 29.2 %all_to_all.60 = bf16[64,2,1,1,8192]{4,1,3,2,0:T(2,128)(2,1)S(1)} all-to-all(bf16[64,2,1,1,8192]{4,1,3,2,0:T(2,128)(2,1)S(1)} %copy.32), channel_id=1, replica_groups=mesh['dp'=4,'freq'=8] {'dp'}, dimensions={0} | all-to-all | bytes 4194304 | tf_op jit(solution)/shard_map/all_to_all | solution.py:98
  139.2 1.2 copy.33
  140.4 1.6 copy.34
  142.0 52.3 %all_to_all.61 = bf16[16,2,4,1,8192]{4,2,1,3,0:T(4,128)(2,1)S(1)} all-to-all(bf16[16,2,4,1,8192]{4,2,1,3,0:T(4,128)(2,1)S(1)} %copy.34), channel_id=1, replica_groups=mesh['dp'=4,'freq'=8] {'freq'}, dimensions={0} | all-to-all | bytes 4194304 | tf_op jit(solution)/shard_map/all_to_all | solution.py:97
  194.3 1.2 multiply_reduce_fusion
  195.6 0.1 reduce_sum.27
  195.7 3.2 %copy.46 = f32[8,2,2,4,1,8192]{5,0,3,1,2,4:T(8,128)} copy(bf16[8,2,2,4,1,8192]{5,3,2,1,0,4:T(4,128)(2,1)S(1)} %bitcast.49) | data formatting | bytes 6291456 | tf_op jit(solution)/shard_map/convert_element_type | solution.py:58
  198.8 5.0 %reshape.259 = f32[2,2,512,512]{3,2,0,1:T(8,128)} reshape(f32[2,2,4,8,1,8192]{5,3,2,0,1,4:T(8,128)} %bitcast.50) | data formatting | bytes 8388608 | tf_op jit(solution)/shard_map/convert_element_type | solution.py:58
  203.8 2.8 multiply_convert_fusion
  206.6 0.1 fusion.83
  206.7 0.1 slice_bitcast_fusion.5
  206.9 2.6 fusion.23
  209.5 0.1 slice_negate_fusion
  209.6 2.6 subtract_convert_fusion
  212.2 0.2 fusion.84
  212.4 0.5 stack.21
  212.9 0.5 stack.22
  213.5 0.2 pad_maximum_fusion.2
  213.7 0.2 copy.42
  213.9 28.2 %all_to_all.62 = bf16[2,2,4,8,8192]{4,3,1,0,2:T(8,128)(2,1)S(1)} all-to-all(bf16[2,2,4,8,8192]{4,3,1,0,2:T(8,128)(2,1)S(1)} %copy.42), channel_id=1, replica_groups=mesh['dp'=4,'freq'=8] {'dp'}, dimensions={2} | all-to-all | bytes 4194304 | tf_op jit(solution)/shard_map/all_to_all | solution.py:112
  242.0 3.5 %copy.39 = bf16[8,2,1,8,8192]{4,1,0,2,3:T(2,128)(2,1)} copy(bf16[8,2,1,8,8192]{4,3,1,0,2:T(8,128)(2,1)S(1)} %bitcast.55) | data formatting | bytes 4194304 | tf_op jit(solution)/shard_map/all_to_all | solution.py:112
  245.6 3.6 %all-to-all-start.3 = ((bf16[8,2,1,8,8192]{4,1,0,2,3:T(2,128)(2,1)}), bf16[8,2,1,8,8192]{4,1,0,2,3:T(2,128)(2,1)S(1)}, u32[]{:S(2)}, u32[]{:S(2)}) async-start(bf16[8,2,1,8,8192]{4,1,0,2,3:T(2,128)(2,1)} %copy.39), calls=%async_computation.4 | async-start | bytes 4194304 | tf_op jit(solution)/shard_map/all_to_all | solution.py:111
  249.2 48.0 %all-to-all-done.3 = bf16[8,2,1,8,8192]{4,1,0,2,3:T(2,128)(2,1)S(1)} async-done(((bf16[8,2,1,8,8192]{4,1,0,2,3:T(2,128)(2,1)}), bf16[8,2,1,8,8192]{4,1,0,2,3:T(2,128)(2,1)S(1)}, u32[]{:S(2)}, u32[]{:S(2)}) %all-to-all-start.3) | async-done | bytes 2097184 | tf_op jit(solution)/shard_map/all_to_all | solution.py:111
  297.2 1.2 copy.48
  298.4 0.8 fusion.28
  299.2 1.8 fusion.3
  (8 shorter events, 0.1 us)
Async XLA Ops:
  6.5 53.4 %reduce-scatter.2.cloned.1.call-start = ((), (), s32[]{:S(2)}) async-start(), calls=%async_computation.5 | async-start | bytes 5242880 | tf_op jit(solution)/shard_map/reduce_scatter | solution.py:86
  12.5 89.8 %copy-start.1 = (f32[27,8192]{1,0:T(8,128)S(1)}, f32[27,8192]{1,0:T(8,128)}, u32[]{:S(2)}) copy-start(f32[27,8192]{1,0:T(8,128)} %param.3) | copy-start | bytes 2654212
  59.9 45.7 %copy-start = (f32[27,1,8192]{2,0,1:T(8,128)S(1)}, f32[27,1,8192]{2,0,1:T(8,128)}, u32[]{:S(2)}) copy-start(f32[27,1,8192]{2,0,1:T(8,128)} %reduce-scatter.2.cloned.1.call-done) | copy-start | bytes 2654212
  245.6 51.7 %all-to-all-start.3 = ((bf16[8,2,1,8,8192]{4,1,0,2,3:T(2,128)(2,1)}), bf16[8,2,1,8,8192]{4,1,0,2,3:T(2,128)(2,1)S(1)}, u32[]{:S(2)}, u32[]{:S(2)}) async-start(bf16[8,2,1,8,8192]{4,1,0,2,3:T(2,128)(2,1)} %copy.39), calls=%async_computation.4 | async-start | bytes 4194304 | tf_op jit(solution)/shard_map/all_to_all | solution.py:111
Sparse Core Ops, SparseCore 0:
  12.7 47.2 reduce-scatter.1
where the time goes:
time: 308 us
  blocking collectives  149 us (48%)
  waiting for transfers between devices  95.4 us (31%)
  local copies, waits for them, and re-layouts  25.4 us (8%)
  between operations  14.3 us (5%)
  matrix products  13 us (4%)
  other arithmetic  6.98 us (2%)
  starting transfers between devices  3.6 us (1%)
    all_to_all x1, blocking collectives, on_device(): lax.all_to_all(lax.all_to_all(spectra.reshape(count, 2, 1, 1, row_width),...  52.3 us
    all_to_all x1, waiting for transfers between devices, on_device(): lax.all_to_all(lax.all_to_all(polar_part.reshape(KD, 2, devices_dp, devic...  48 us
    reduce_scatter x1, waiting for transfers between devices, on_device(): lax.psum_scatter(grad_parts[0], 'dp', scatter_dimension=1, tiled=True)  47.3 us
    psum x1, blocking collectives, clip_factor(): summed = lax.psum(local_square, ('dp', 'freq'))  39.5 us
    all_to_all x1, blocking collectives, on_device(): lax.all_to_all(spectra.reshape(count, 2, 1, 1, row_width), 'dp', split_ax...  29.2 us
    all_to_all x1, blocking collectives, on_device(): lax.all_to_all(polar_part.reshape(KD, 2, devices_dp, devices_freq, row_wi...  28.2 us
    convert_element_type x2, local copies, waits for them, and re-layouts, polar_step(): spectra.astype(jnp.float32)  8.14 us
  transfers between devices with their start and end apart: 2, of which 2 were waited for; matrix products, arithmetic and copies ran while one was open for 0% of the time, Pallas kernels for 0%

commit v1 on v0

--- a/solution.py
+++ b/solution.py
@@ -12,6 +12,28 @@
 KD = 2
 CLIP = 0.25
 HIGH = lax.Precision.HIGHEST
+
+
+def split_up(x, dim, length):
+    before, after = (x.shape[:dim], x.shape[dim + 1 :])
+    return jnp.moveaxis(x.reshape(*before, length, -1, *after), dim, 0)
+
+
+def in_order(blocks, dim):
+    blocks = jnp.moveaxis(blocks, 0, dim)
+    shape = blocks.shape
+    return blocks.reshape(*shape[:dim], shape[dim] * shape[dim + 1], *shape[dim + 2 :])
+
+
+def swapped_with_each(x, axis, split_dim, concat_dim):
+    devices, mine = (lax.axis_size(axis), lax.axis_index(axis))
+    parts = split_up(x, split_dim, devices)
+    outs = [parts[mine]]
+    for step in range(1, devices):
+        sent = parts[mine ^ step]
+        outs.append(lax.ppermute(sent, axis, [(i, i ^ step) for i in range(devices)]))
+    parts = jnp.stack(outs)[mine ^ jnp.arange(devices)]
+    return in_order(parts, concat_dim)
 
 
 def tap_phases(freq_ids, stride):
@@ -94,7 +116,7 @@
     spectra = spectrum(kernel_all - factor * gradient_all, cosine, sine_rows)
     spectra = spectra.astype(jnp.bfloat16)
     count, row_width = (spectra.shape[0], spectra.shape[2])
-    whole = lax.all_to_all(
+    whole = swapped_with_each(
         lax.all_to_all(
             spectra.reshape(count, 2, 1, 1, row_width),
             "dp",
@@ -103,9 +125,8 @@
             tiled=True,
         ),
         "freq",
-        split_axis=0,
-        concat_axis=3,
-        tiled=True,
+        0,
+        3,
     )
     polar_part = polar_step(whole.reshape(KD, 2, C, C))
     returned = lax.all_to_all(

time: 308 us -> 318 us (1.032)
  blocking collectives: 149 us -> 67.7 us
  waiting for transfers between devices: 95.4 us -> 159 us
  starting transfers between devices: 3.6 us -> 20.9 us
  local copies, waits for them, and re-layouts: 25.4 us -> 34.9 us
    all_to_all x2 -> x0, blocking collectives: 81.6 us -> none  [the longest x1 52.3 us: on_device(): lax.all_to_all(lax.all_to_all(spectra.reshape(count, 2, 1, 1, row_width),...]
    ppermute x0 -> x7, waiting for transfers between devices: none -> 37.9 us  [swapped_with_each(): lax.ppermute(sent, axis, [(i, i ^ step) for i in range(devices)])]
    all_to_all x0 -> x1, waiting for transfers between devices: none -> 25.6 us  [on_device(): lax.all_to_all(spectra.reshape(count, 2, 1, 1, row_width), 'dp', split_ax...]
    ppermute x0 -> x7, starting transfers between devices: none -> 13.5 us  [swapped_with_each(): lax.ppermute(sent, axis, [(i, i ^ step) for i in range(devices)])]
    gather x0 -> x1, local copies, waits for them, and re-layouts: none -> 3.95 us  [swapped_with_each(): parts = jnp.stack(outs)[mine ^ jnp.arange(devices)]]
    all_to_all x0 -> x1, starting transfers between devices: none -> 3.79 us  [on_device(): lax.all_to_all(spectra.reshape(count, 2, 1, 1, row_width), 'dp', split_ax...]
    unnamed x5 -> x13, local copies, waits for them, and re-layouts: 5.99 us -> 8.05 us
  transfers between devices with their start and end apart: 2 -> 10, of which waited for: 2 -> 6; matrix products, arithmetic and copies ran while one was open for 0% -> 0% of each run, Pallas kernels for 0% -> 0%
where the time goes in v1:
time: 318 us; the launch traced here: 317 us
  waiting for transfers between devices  159 us (50%)
  blocking collectives  67.7 us (21%)
  local copies, waits for them, and re-layouts  34.9 us (11%)
  starting transfers between devices  20.9 us (7%)
  between operations  14.4 us (5%)
  matrix products  13 us (4%)
  other arithmetic  7.42 us (2%)
    all_to_all x1, waiting for transfers between devices, on_device(): lax.all_to_all(lax.all_to_all(polar_part.reshape(KD, 2, devices_dp, devic...  48 us
    reduce_scatter x1, waiting for transfers between devices, on_device(): lax.psum_scatter(grad_parts[0], 'dp', scatter_dimension=1, tiled=True)  47.3 us
    psum x1, blocking collectives, clip_factor(): summed = lax.psum(local_square, ('dp', 'freq'))  39.5 us
    ppermute x7, waiting for transfers between devices, swapped_with_each(): lax.ppermute(sent, axis, [(i, i ^ step) for i in range(devices)])  37.9 us
    all_to_all x1, blocking collectives, on_device(): lax.all_to_all(polar_part.reshape(KD, 2, devices_dp, devices_freq, row_wi...  28.2 us
    all_to_all x1, waiting for transfers between devices, on_device(): lax.all_to_all(spectra.reshape(count, 2, 1, 1, row_width), 'dp', split_ax...  25.6 us
    ppermute x7, starting transfers between devices, swapped_with_each(): lax.ppermute(sent, axis, [(i, i ^ step) for i in range(devices)])  13.5 us
    convert_element_type x2, local copies, waits for them, and re-layouts, polar_step(): spectra.astype(jnp.float32)  9.35 us
  transfers between devices with their start and end apart: 10, of which 6 were waited for; matrix products, arithmetic and copies ran while one was open for 0% of the time, Pallas kernels for 0%

profile of v1, /device:TPU:0, one launch (start us, length us, event | category | flops | bytes accessed | tf_op | source)
XLA Modules:
  0.0 317.2 jit_solution(2661396727386740311)
XLA Ops:
  6.5 0.0 reduce-scatter.2.cloned.1.call-start
  6.5 6.0 %copy.45 = f32[1,27,4,8192]{3,1,2,0:T(8,128)} copy(f32[1,27,4,8192]{3,2,1,0:T(4,128)} %param.2) | data formatting | bytes 7077888 | tf_op args[0]
  12.5 0.0 copy-start.1
  12.5 0.0 reduce-scatter.2.cloned.1.call-update
  12.6 47.3 %reduce-scatter.2.cloned.1.call-done = f32[27,1,8192]{2,0,1:T(8,128)} async-done(((f32[27,4,8192]{2,0,1:T(8,128)}), f32[27,1,8192]{2,0,1:T(8,128)}) %reduce-scatter.2.cloned.1.call-update) | async-done | bytes 884752 | tf_op jit(solution)/shard_map/reduce_scatter | solution.py:108
  59.9 0.0 copy-start
  60.0 2.2 multiply_reduce_fusion
  62.1 39.5 %psum.7 = f32[]{:T(128)} all-reduce(f32[]{:T(128)} %multiply_reduce_fusion), channel_id=1, replica_groups=mesh['dp'=4,'freq'=8] {'dp','freq'}, use_global_device_ids=true, to_apply=%region_2.3 | all-reduce | flops 1 | bytes 8 | tf_op jit(solution)/shard_map/psum | solution.py:59
  102.3 0.0 copy-done.1
  102.4 3.2 %fusion.2 = bf16[64,1,1,1,8192]{4,0,3,2,1:T(8,128)(2,1)S(1)} fusion(f32[27,8192]{1,0:T(8,128)S(1)} %copy-done.1, f32[27,1,8192]{2,0,1:T(8,128)} %reduce-scatter.2.cloned.1.call-done, f32[]{:T(128)S(6)} %min_shard_map.3, s32[64]{0:T(128)S(1)} %get-tuple-element.19, s32[64]{0:T(128)S(1)} %get-tuple-element.20, s32[64]{0:T(128)S(1)} %and_select_fusion.3, ...), kind=kOutput, calls=%fused_computation.5 | convolution fusion | flops 171396544 | bytes 2819144 | tf_op jit(solution)/shard_map/dot_general | solution.py:65
  105.6 0.0 copy-done
  105.6 2.0 fusion.1
  107.6 0.2 pad_maximum_fusion
  107.8 3.5 %copy.32 = bf16[64,2,1,1,8192]{4,1,3,2,0:T(2,128)(2,1)} copy(bf16[64,2,1,1,8192]{4,0,3,2,1:T(8,128)(2,1)S(1)} %pad_maximum_fusion) | data formatting | bytes 4194304 | tf_op jit(solution)/shard_map/stack | solution.py:66
  111.3 3.8 %all-to-all-start = ((bf16[64,2,1,1,8192]{4,1,3,2,0:T(2,128)(2,1)}), bf16[64,2,1,1,8192]{4,1,3,2,0:T(2,128)(2,1)S(1)}, u32[]{:S(2)}, u32[]{:S(2)}) async-start(bf16[64,2,1,1,8192]{4,1,3,2,0:T(2,128)(2,1)} %copy.32), calls=%async_computation.1 | async-start | bytes 4194304 | tf_op jit(solution)/shard_map/all_to_all | solution.py:120
  115.1 25.6 %all-to-all-done = bf16[64,2,1,1,8192]{4,1,3,2,0:T(2,128)(2,1)S(1)} async-done(((bf16[64,2,1,1,8192]{4,1,3,2,0:T(2,128)(2,1)}), bf16[64,2,1,1,8192]{4,1,3,2,0:T(2,128)(2,1)S(1)}, u32[]{:S(2)}, u32[]{:S(2)}) %all-to-all-start) | async-done | bytes 2097184 | tf_op jit(solution)/shard_map/all_to_all | solution.py:120
  140.7 1.2 copy.33
  141.9 1.6 copy.34
  143.5 0.9 dynamic-slice_bitcast_fusion
  144.4 2.2 collective-permute-start
  146.6 1.8 collective-permute-start.6
  148.4 1.6 collective-permute-start.5
  150.0 1.9 collective-permute-start.4
  151.9 2.4 collective-permute-start.3
  154.3 3.6 %collective-permute-done = bf16[2,2,4,1,8192]{4,2,1,0,3:T(4,128)(2,1)S(1)} collective-permute-done((bf16[2,2,4,1,8192]{4,2,1,0,3:T(4,128)(2,1)S(1)}, bf16[2,2,4,1,8192]{4,2,1,0,3:T(4,128)(2,1)S(1)}, u32[]{:S(2)}, u32[]{:S(2)}) %collective-permute-start) | collective-permute-done | bytes 262176 | tf_op jit(solution)/shard_map/ppermute | solution.py:34
  158.0 0.0 collective-permute-start.1
  158.0 0.1 bitcast_dynamic-update-slice_fusion.6
  158.1 18.2 %collective-permute-done.1 = bf16[2,2,4,1,8192]{4,2,1,0,3:T(4,128)(2,1)S(1)} collective-permute-done((bf16[2,2,4,1,8192]{4,2,1,0,3:T(4,128)(2,1)S(1)}, bf16[2,2,4,1,8192]{4,2,1,0,3:T(4,128)(2,1)S(1)}, u32[]{:S(2)}, u32[]{:S(2)}) %collective-permute-start.1) | collective-permute-done | bytes 262176 | tf_op jit(solution)/shard_map/ppermute | solution.py:34
  176.3 3.6 %collective-permute-start.2 = (bf16[2,2,4,1,8192]{4,2,1,0,3:T(4,128)(2,1)S(1)}, bf16[2,2,4,1,8192]{4,2,1,0,3:T(4,128)(2,1)S(1)}, u32[]{:S(2)}, u32[]{:S(2)}) collective-permute-start(bf16[2,2,4,1,8192]{4,2,1,0,3:T(4,128)(2,1)S(1)} %get-tuple-element.15), channel_id=1, source_target_pairs={{0,3},{1,2},{2,1},{3,0},{4,7},{5,6},{6,5},{7,4},{8,11},{9,10},{10,... | collective-permute-start | bytes 786440 | tf_op jit(solution)/shard_map/ppermute | solution.py:34
  179.9 0.1 bitcast_dynamic-update-slice_fusion.5
  180.0 16.1 %collective-permute-done.2 = bf16[2,2,4,1,8192]{4,2,1,0,3:T(4,128)(2,1)S(1)} collective-permute-done((bf16[2,2,4,1,8192]{4,2,1,0,3:T(4,128)(2,1)S(1)}, bf16[2,2,4,1,8192]{4,2,1,0,3:T(4,128)(2,1)S(1)}, u32[]{:S(2)}, u32[]{:S(2)}) %collective-permute-start.2) | collective-permute-done | bytes 262176 | tf_op jit(solution)/shard_map/ppermute | solution.py:34
  196.1 0.1 bitcast_dynamic-update-slice_fusion.4
  196.2 0.0 collective-permute-done.3
  196.2 0.1 bitcast_dynamic-update-slice_fusion.3
  196.3 0.0 collective-permute-done.4
  196.4 0.1 bitcast_dynamic-update-slice_fusion.2
  196.5 0.0 collective-permute-done.5
  196.5 0.1 bitcast_dynamic-update-slice_fusion.1
  196.6 0.0 collective-permute-done.6
  196.6 0.1 bitcast_dynamic-update-slice_fusion
  196.7 1.3 copy-done.2
  198.1 4.0 %gather_fusion = bf16[8,2,2,4,8192]{4,3,2,1,0:T(4,128)(2,1)S(1)} fusion(bf16[8,2,2,4,8192]{4,3,2,1,0:T(4,128)(2,1)} %bitcast.86, s32[1024]{0:T(1024)S(1)} %pad_clamp_fusion), kind=kCustom, calls=%fused_computation | custom fusion | bytes 4194336 | tf_op jit(solution)/shard_map/gather | solution.py:35
  202.0 1.2 fusion.4
  203.2 0.5 convert_bitcast_fusion
  203.8 4.4 %copy.35 = f32[2,2,4,8,1,8192]{5,3,2,0,1,4:T(8,128)} copy(f32[2,2,4,8,1,8192]{5,2,1,0,3,4:T(4,128)S(1)} %convert_bitcast_fusion) | data formatting | bytes 8388608 | tf_op jit(solution)/shard_map/convert_element_type | solution.py:80
  208.1 5.0 %reshape.272 = f32[2,2,512,512]{3,2,0,1:T(8,128)} reshape(f32[2,2,4,8,1,8192]{5,3,2,0,1,4:T(8,128)} %copy.35) | data formatting | bytes 8388608 | tf_op jit(solution)/shard_map/convert_element_type | solution.py:80
  213.1 2.8 multiply_convert_fusion
  215.9 0.1 fusion.85
  216.0 0.1 slice_bitcast_fusion.5
  216.1 2.6 fusion.24
  218.8 0.1 slice_negate_fusion
  218.9 2.6 subtract_convert_fusion
  221.5 0.2 fusion.86
  221.7 0.5 stack.53
  222.2 0.5 stack.54
  222.8 0.2 pad_maximum_fusion.2
  223.0 0.2 copy.42
  223.2 28.2 %all_to_all.48 = bf16[2,2,4,8,8192]{4,3,1,0,2:T(8,128)(2,1)S(1)} all-to-all(bf16[2,2,4,8,8192]{4,3,1,0,2:T(8,128)(2,1)S(1)} %copy.42), channel_id=1, replica_groups=mesh['dp'=4,'freq'=8] {'dp'}, dimensions={2} | all-to-all | bytes 4194304 | tf_op jit(solution)/shard_map/all_to_all | solution.py:133
  251.3 3.5 %copy.39 = bf16[8,2,1,8,8192]{4,1,0,2,3:T(2,128)(2,1)} copy(bf16[8,2,1,8,8192]{4,3,1,0,2:T(8,128)(2,1)S(1)} %bitcast.85) | data formatting | bytes 4194304 | tf_op jit(solution)/shard_map/all_to_all | solution.py:133
  254.8 3.6 %all-to-all-start.2 = ((bf16[8,2,1,8,8192]{4,1,0,2,3:T(2,128)(2,1)}), bf16[8,2,1,8,8192]{4,1,0,2,3:T(2,128)(2,1)S(1)}, u32[]{:S(2)}, u32[]{:S(2)}) async-start(bf16[8,2,1,8,8192]{4,1,0,2,3:T(2,128)(2,1)} %copy.39), calls=%async_computation.3 | async-start | bytes 4194304 | tf_op jit(solution)/shard_map/all_to_all | solution.py:132
  258.5 48.0 %all-to-all-done.2 = bf16[8,2,1,8,8192]{4,1,0,2,3:T(2,128)(2,1)S(1)} async-done(((bf16[8,2,1,8,8192]{4,1,0,2,3:T(2,128)(2,1)}), bf16[8,2,1,8,8192]{4,1,0,2,3:T(2,128)(2,1)S(1)}, u32[]{:S(2)}, u32[]{:S(2)}) %all-to-all-start.2) | async-done | bytes 2097184 | tf_op jit(solution)/shard_map/all_to_all | solution.py:132
  306.5 1.2 copy.46
  307.7 0.8 fusion.29
  308.5 1.8 fusion.3
  (10 shorter events, 0.1 us)
Async XLA Ops:
  6.5 53.4 %reduce-scatter.2.cloned.1.call-start = ((), (), s32[]{:S(2)}) async-start(), calls=%async_computation.4 | async-start | bytes 5242880 | tf_op jit(solution)/shard_map/reduce_scatter | solution.py:108
  12.5 89.8 %copy-start.1 = (f32[27,8192]{1,0:T(8,128)S(1)}, f32[27,8192]{1,0:T(8,128)}, u32[]{:S(2)}) copy-start(f32[27,8192]{1,0:T(8,128)} %param.3) | copy-start | bytes 2654212
  59.9 45.6 %copy-start = (f32[27,1,8192]{2,0,1:T(8,128)S(1)}, f32[27,1,8192]{2,0,1:T(8,128)}, u32[]{:S(2)}) copy-start(f32[27,1,8192]{2,0,1:T(8,128)} %reduce-scatter.2.cloned.1.call-done) | copy-start | bytes 2654212
  111.3 29.4 %all-to-all-start = ((bf16[64,2,1,1,8192]{4,1,3,2,0:T(2,128)(2,1)}), bf16[64,2,1,1,8192]{4,1,3,2,0:T(2,128)(2,1)S(1)}, u32[]{:S(2)}, u32[]{:S(2)}) async-start(bf16[64,2,1,1,8192]{4,1,3,2,0:T(2,128)(2,1)} %copy.32), calls=%async_computation.1 | async-start | bytes 4194304 | tf_op jit(solution)/shard_map/all_to_all | solution.py:120
  144.4 13.6 %collective-permute-start = (bf16[2,2,4,1,8192]{4,2,1,0,3:T(4,128)(2,1)S(1)}, bf16[2,2,4,1,8192]{4,2,1,0,3:T(4,128)(2,1)S(1)}, u32[]{:S(2)}, u32[]{:S(2)}) collective-permute-start(bf16[2,2,4,1,8192]{4,2,1,0,3:T(4,128)(2,1)S(1)} %get-tuple-element.17), channel_id=1, source_target_pairs={{0,1},{1,0},{2,3},{3,2},{4,5},{5,4},{6,7},{7,6},{8,9},{9,8},{10,11... | collective-permute-start | bytes 786440 | tf_op jit(solution)/shard_map/ppermute | solution.py:34
  146.6 50.0 %collective-permute-start.6 = (bf16[2,2,4,1,8192]{4,2,1,0,3:T(4,128)(2,1)S(1)}, bf16[2,2,4,1,8192]{4,2,1,0,3:T(4,128)(2,1)S(1)}, u32[]{:S(2)}, u32[]{:S(2)}) collective-permute-start(bf16[2,2,4,1,8192]{4,2,1,0,3:T(4,128)(2,1)S(1)} %get-tuple-element.11), channel_id=1, source_target_pairs={{0,7},{1,6},{2,5},{3,4},{4,3},{5,2},{6,1},{7,0},{8,15},{9,14},{10,... | collective-permute-start | bytes 786440 | tf_op jit(solution)/shard_map/ppermute | solution.py:34
  148.4 48.1 %collective-permute-start.5 = (bf16[2,2,4,1,8192]{4,2,1,0,3:T(4,128)(2,1)S(1)}, bf16[2,2,4,1,8192]{4,2,1,0,3:T(4,128)(2,1)S(1)}, u32[]{:S(2)}, u32[]{:S(2)}) collective-permute-start(bf16[2,2,4,1,8192]{4,2,1,0,3:T(4,128)(2,1)S(1)} %get-tuple-element.12), channel_id=1, source_target_pairs={{0,6},{1,7},{2,4},{3,5},{4,2},{5,3},{6,0},{7,1},{8,14},{9,15},{10,... | collective-permute-start | bytes 786440 | tf_op jit(solution)/shard_map/ppermute | solution.py:34
  150.0 46.4 %collective-permute-start.4 = (bf16[2,2,4,1,8192]{4,2,1,0,3:T(4,128)(2,1)S(1)}, bf16[2,2,4,1,8192]{4,2,1,0,3:T(4,128)(2,1)S(1)}, u32[]{:S(2)}, u32[]{:S(2)}) collective-permute-start(bf16[2,2,4,1,8192]{4,2,1,0,3:T(4,128)(2,1)S(1)} %get-tuple-element.13), channel_id=1, source_target_pairs={{0,5},{1,4},{2,7},{3,6},{4,1},{5,0},{6,3},{7,2},{8,13},{9,12},{10,... | collective-permute-start | bytes 786440 | tf_op jit(solution)/shard_map/ppermute | solution.py:34
  151.9 44.3 %collective-permute-start.3 = (bf16[2,2,4,1,8192]{4,2,1,0,3:T(4,128)(2,1)S(1)}, bf16[2,2,4,1,8192]{4,2,1,0,3:T(4,128)(2,1)S(1)}, u32[]{:S(2)}, u32[]{:S(2)}) collective-permute-start(bf16[2,2,4,1,8192]{4,2,1,0,3:T(4,128)(2,1)S(1)} %get-tuple-element.14), channel_id=1, source_target_pairs={{0,4},{1,5},{2,6},{3,7},{4,0},{5,1},{6,2},{7,3},{8,12},{9,13},{10,... | collective-permute-start | bytes 786440 | tf_op jit(solution)/shard_map/ppermute | solution.py:34
  158.0 18.3 %collective-permute-start.1 = (bf16[2,2,4,1,8192]{4,2,1,0,3:T(4,128)(2,1)S(1)}, bf16[2,2,4,1,8192]{4,2,1,0,3:T(4,128)(2,1)S(1)}, u32[]{:S(2)}, u32[]{:S(2)}) collective-permute-start(bf16[2,2,4,1,8192]{4,2,1,0,3:T(4,128)(2,1)S(1)} %get-tuple-element.16), channel_id=1, source_target_pairs={{0,2},{1,3},{2,0},{3,1},{4,6},{5,7},{6,4},{7,5},{8,10},{9,11},{10,... | collective-permute-start | bytes 786440 | tf_op jit(solution)/shard_map/ppermute | solution.py:34
  176.3 19.8 %collective-permute-start.2 = (bf16[2,2,4,1,8192]{4,2,1,0,3:T(4,128)(2,1)S(1)}, bf16[2,2,4,1,8192]{4,2,1,0,3:T(4,128)(2,1)S(1)}, u32[]{:S(2)}, u32[]{:S(2)}) collective-permute-start(bf16[2,2,4,1,8192]{4,2,1,0,3:T(4,128)(2,1)S(1)} %get-tuple-element.15), channel_id=1, source_target_pairs={{0,3},{1,2},{2,1},{3,0},{4,7},{5,6},{6,5},{7,4},{8,11},{9,10},{10,... | collective-permute-start | bytes 786440 | tf_op jit(solution)/shard_map/ppermute | solution.py:34
  196.7 1.3 copy-start.2
  254.8 51.7 %all-to-all-start.2 = ((bf16[8,2,1,8,8192]{4,1,0,2,3:T(2,128)(2,1)}), bf16[8,2,1,8,8192]{4,1,0,2,3:T(2,128)(2,1)S(1)}, u32[]{:S(2)}, u32[]{:S(2)}) async-start(bf16[8,2,1,8,8192]{4,1,0,2,3:T(2,128)(2,1)} %copy.39), calls=%async_computation.3 | async-start | bytes 4194304 | tf_op jit(solution)/shard_map/all_to_all | solution.py:132
Sparse Core Ops, SparseCore 0:
  12.7 47.2 reduce-scatter.1
